TPU v7x, 128 devices: a whole 4x4x4 slice. The times are simulated.
128 devices in a mesh: grp: 8 (over y, core), shard: 16 (over z, x).
Axes of the slice: x: 4, y: 4, z: 4, core: 2. Of those that a mesh axis runs over, the one named last changes fastest.
Arguments:
- tokens: bfloat16 [65536, 2560], P(('grp', 'shard')), may hold values from -6 to 6
- gain: float32 [2560], replicated, may hold values from 0.25 to 1.75
- w_qkv: bfloat16 [2560, 3072], P(None, 'shard'), may hold values from -1 to 1
- prefix_kv: bfloat16 [8, 2048, 512], P('grp', 'shard'), may hold values from -6 to 6
- prefix_owner: int32 [8], P('grp'), may hold values from 0 to 7, as said below
- suffix_len: int32 [8, 16], P('grp', 'shard'), may hold values from 1 to 512, 5120 in all within a row
- slots: int32 [8, 8192], P('grp', 'shard'), may hold values from 0 to 8191, as said below
Outputs:
- attended: bfloat16 [65536, 2560], P(('grp', 'shard'))
Inputs may be any that keep to these rules, and one draw needn't show every extreme that they name: In each group the slots are a permutation of 0 to 8191; in each aligned run of 512 entries the k-th block of 32 entries holds slots k * 512 to (k + 1) * 512 - 1. `suffix_len`: each group's lengths sum to 5120 and one of them equals 512. `prefix_owner`: each entry names one of the 8 caches; several groups may name the same one.
All inputs are finite; a program needn't handle non-finite values.
Results may differ from a plain program's by a relative error of at most 0.0069.
Values may be sent and summed in bfloat16 or wider, within the bound.
No kernel may reach another device: no remote copies, remote signals or barrier semaphores. Data moves between devices by JAX's collectives and lax.ppermute only.
A program may use at most 128 MiB of HBM per device.

v0:
```python
import jax
import jax.numpy as jnp
from jax import lax
from jax.sharding import PartitionSpec as P

H = 10
HD = 256
WINDOW = 2048
SUF = 512
HQ = 2560


def normalize(rows, gain):
    rows32 = rows.astype(jnp.float32)
    factor = lax.rsqrt(jnp.mean(rows32 * rows32, axis=-1, keepdims=True) + 1e-06)
    return (rows32 * factor * gain).astype(jnp.bfloat16)


def attend_request(queries, suffix_kv, prefix, length):
    keys = jnp.concatenate([prefix[:, :HD], suffix_kv[:, :HD]], axis=0)
    values = jnp.concatenate([prefix[:, HD:], suffix_kv[:, HD:]], axis=0)
    span = keys.shape[0]
    prefix_len = prefix.shape[0]
    count = queries.shape[0]
    query_pos = jnp.arange(count, dtype=jnp.int32)[:, None]
    key_pos = jnp.arange(span, dtype=jnp.int32)[None, :]
    visible = (
        (key_pos > prefix_len + query_pos - WINDOW)
        & (key_pos <= prefix_len + query_pos)
        & (key_pos < prefix_len + length)
    )
    heads = queries.reshape(count, H, HD).transpose(1, 0, 2)

    def one_head(head_q):
        scores = jnp.dot(head_q, keys.T, preferred_element_type=jnp.float32) * HD ** (-0.5)
        scores = jnp.where(visible, scores, -1e30)
        top = jnp.max(scores, axis=-1, keepdims=True)
        expd = jnp.exp(scores - top)
        weights = (expd / jnp.sum(expd, axis=-1, keepdims=True)).astype(jnp.bfloat16)
        return jnp.dot(weights, values, preferred_element_type=jnp.float32)

    result = lax.map(one_head, heads).transpose(1, 0, 2).reshape(count, H * HD)
    return jnp.where(query_pos < length, result, 0.0).astype(jnp.bfloat16)


def shards(tokens, gain, w_qkv, prefix_kv, prefix_owner, suffix_len, slots):
    tok_dev = tokens.shape[0]
    order = slots.reshape(tok_dev)
    normed = normalize(tokens, gain)
    projected = jnp.dot(
        normed,
        lax.all_gather(w_qkv, "shard", axis=1, tiled=True),
        preferred_element_type=jnp.float32,
    ).astype(jnp.bfloat16)
    arrived, order = (
        lax.all_to_all(projected, "shard", split_axis=0, concat_axis=0, tiled=True),
        lax.all_to_all(order, "shard", split_axis=0, concat_axis=0, tiled=True),
    )
    first_slot = lax.axis_index("shard") * tok_dev
    placed = jnp.zeros_like(arrived).at[order - first_slot].set(arrived)
    owner = prefix_owner[0]
    sliced = lax.all_gather(prefix_kv, "grp", axis=0, tiled=True)
    chosen = lax.dynamic_index_in_dim(sliced, owner, 0, keepdims=False)
    prefix = lax.all_gather(chosen, "shard", axis=0, tiled=True)
    lengths = suffix_len.reshape(-1)
    req_count = lengths.shape[0]
    blocks = placed.reshape(req_count, SUF, placed.shape[1])
    results = attend_request(blocks[0, :, :HQ], blocks[0, :, HQ:], prefix, lengths[0])
    return results


def solution(mesh):
    return jax.shard_map(
        shards,
        mesh=mesh,
        in_specs=(
            P(("grp", "shard"), None),
            P(),
            P(None, "shard"),
            P("grp", "shard", None),
            P("grp"),
            P("grp", "shard"),
            P("grp", "shard"),
        ),
        out_specs=P(("grp", "shard"), None),
        check_vma=False,
    )
```

profile of v0, /device:TPU:0, one launch (start us, length us, event | category | flops | bytes accessed | tf_op | source)
XLA Modules:
  0.0 314.0 jit_solution(14929914385447946524)
XLA Ops:
  6.5 0.7 all-gather.7.cloned.1.call-update
  7.3 0.7 all-gather.5.cloned.1.call-update
  8.0 0.5 broadcast.76
  8.5 1.3 reduce.7
  9.9 0.7 all_to_all.14
  10.6 8.0 %all-to-all-start = ((s32[16,32,1]{1,2,0:T(1,128)}), s32[16,32,1]{1,2,0:T(1,128)S(1)}, u32[]{:S(2)}, u32[]{:S(2)}) async-start(s32[16,32,1]{1,2,0:T(1,128)} %all_to_all.14), calls=%async_computation | async-start | bytes 16384 | tf_op jit(solution)/shard_map/all_to_all | solution.py:57
  19.3 2.4 fusion.11
  21.6 13.2 %all-gather.7.cloned.1.call-done = bf16[8,128,512]{2,1,0:T(8,128)(2,1)} async-done(((bf16[1,128,512]{2,1,0:T(8,128)(2,1)}), bf16[8,128,512]{2,1,0:T(8,128)(2,1)}) %all-gather.7.cloned.1.call-update) | async-done | bytes 1048592 | tf_op jit(solution)/shard_map/all_gather | solution.py:62
  34.8 1.6 constant_dynamic-slice_fusion
  36.4 106.5 %all-gather.5.cloned.1.call-done = bf16[2560,3072]{0,1:T(8,128)(2,1)} async-done(((bf16[2560,192]{0,1:T(8,128)(2,1)}), bf16[2560,3072]{0,1:T(8,128)(2,1)}) %all-gather.5.cloned.1.call-update) | async-done | bytes 15728656 | tf_op jit(solution)/shard_map/all_gather | solution.py:52
  143.0 13.0 %convolution_convert_fusion = bf16[512,3072]{1,0:T(8,128)(2,1)} fusion(bf16[2560,3072]{0,1:T(8,128)(2,1)} %all-gather.5.cloned.1.call-done, bf16[512,2560]{1,0:T(8,128)(2,1)S(1)} %copy-done.3, f32[2560]{0:T(1024)S(1)} %copy-done.5, f32[512]{0:T(512)S(1)} %add_rsqrt_fusion), kind=kOutput, calls=%fused_computation.23 | convolution fusion | flops 8059879424 | bytes 21508096 | tf_op jit(solution)/shard_map/dot_general | solution.py:50
  156.0 5.3 %all-to-all-start.1 = ((bf16[16,32,3072]{2,1,0:T(8,128)(2,1)}), bf16[16,32,3072]{2,1,0:T(8,128)(2,1)S(1)}, u32[]{:S(2)}, u32[]{:S(2)}) async-start(bf16[16,32,3072]{2,1,0:T(8,128)(2,1)} %bitcast.2), calls=%async_computation.1 | async-start | bytes 6291456 | tf_op jit(solution)/shard_map/all_to_all | solution.py:56
  162.0 0.1 sub.27
  162.1 53.2 %all-gather.9.cloned.1.call-done = bf16[1,2048,512]{2,1,0:T(8,128)(2,1)} async-done(((bf16[1,128,512]{2,1,0:T(8,128)(2,1)}), bf16[1,2048,512]{2,1,0:T(8,128)(2,1)}) %all-gather.9.cloned.1.call-update) | async-done | bytes 2097168 | tf_op jit(solution)/shard_map/all_gather | solution.py:64
  215.2 3.0 fusion.21
  218.3 1.6 copy-done.2
  219.9 7.3 %scatter_custom_fusion = bf16[512,3072]{1,0:T(8,128)(2,1)S(1)} fusion(s32[512]{0:T(512)S(1)} %bitcast.50, bf16[512,3072]{1,0:T(8,128)(2,1)} %bitcast.47, bf16[]{:T(256)} %constant.11.clone.1), kind=kCustom, calls=%fused_computation.26 | custom fusion | bytes 3146240 | tf_op jit(solution)/shard_map/scatter | solution.py:60
  227.3 1.7 slice.24
  229.0 0.8 fusion.22
  229.8 4.5 %copy.20 = bf16[1,512,2560]{1,2,0:T(8,128)(2,1)} copy(bf16[1,512,2560]{2,1,0:T(8,128)(2,1)} %slice.24) | data formatting | bytes 5242880 | tf_op jit(solution)/shard_map/slice | solution.py:68
  234.3 2.3 pad_maximum_fusion
  236.6 65.9 %while.11 = (s32[]{:T(128)}, bf16[10,512,256]{1,2,0:T(8,128)(2,1)}, bf16[10,512,256]{1,2,0:T(8,128)(2,1)}, bf16[2560,256]{1,0:T(8,128)(2,1)S(1)}, bf16[2560,256]...) while((s32[]{:T(128)}, bf16[10,512,256]{1,2,0:T(8,128)(2,1)}, ...), condition=%wide.region_5.6_spmd.clone, body=%wide.region_2.5_spmd.clone.sunk | while | flops 1357904896 | bytes 24395376 | solution.py:42
  236.6 3.2 %fusion.33 = (f32[512]{0:T(512)S(1)}, f32[512,2560]{1,0:T(8,128)S(1)}) fusion(bf16[2560,256]{1,0:T(8,128)(2,1)S(1)} %get-tuple-element.165, bf16[10,512,256]{1,2,0:T(8,128)(2,1)} %get-tuple-element.164, s32[]{:T(128)} %get-tuple-element.154, pred[2560]{0:T(1024)(128)(4,1)S(1)} %get-tuple-element.168, s32[512]{0:T(512)S(1)} %get-tuple-element.167), kind=kOutput, calls=%fused_computation.38.clone.1 | convolution fusion | flops 680263168 | bytes 6822912 | tf_op jit(solution)/shard_map/while/body/eval_jaxpr/dot_general | solution.py:35
  239.8 0.8 fusion.34
  240.7 0.5 copy-done.4
  241.1 2.0 fusion.35
  243.2 3.2 %fusion.33 = (f32[512]{0:T(512)S(1)}, f32[512,2560]{1,0:T(8,128)S(1)}) fusion(bf16[2560,256]{1,0:T(8,128)(2,1)S(1)} %get-tuple-element.165, bf16[10,512,256]{1,2,0:T(8,128)(2,1)} %get-tuple-element.164, s32[]{:T(128)} %get-tuple-element.154, pred[2560]{0:T(1024)(128)(4,1)S(1)} %get-tuple-element.168, s32[512]{0:T(512)S(1)} %get-tuple-element.167), kind=kOutput, calls=%fused_computation.38.clone.1 | convolution fusion | flops 680263168 | bytes 6822912 | tf_op jit(solution)/shard_map/while/body/eval_jaxpr/dot_general | solution.py:35
  246.4 0.8 fusion.34
  247.3 0.5 copy-done.4
  247.7 2.0 fusion.35
  249.8 3.2 %fusion.33 = (f32[512]{0:T(512)S(1)}, f32[512,2560]{1,0:T(8,128)S(1)}) fusion(bf16[2560,256]{1,0:T(8,128)(2,1)S(1)} %get-tuple-element.165, bf16[10,512,256]{1,2,0:T(8,128)(2,1)} %get-tuple-element.164, s32[]{:T(128)} %get-tuple-element.154, pred[2560]{0:T(1024)(128)(4,1)S(1)} %get-tuple-element.168, s32[512]{0:T(512)S(1)} %get-tuple-element.167), kind=kOutput, calls=%fused_computation.38.clone.1 | convolution fusion | flops 680263168 | bytes 6822912 | tf_op jit(solution)/shard_map/while/body/eval_jaxpr/dot_general | solution.py:35
  253.0 0.8 fusion.34
  253.9 0.5 copy-done.4
  254.3 2.0 fusion.35
  256.4 3.2 %fusion.33 = (f32[512]{0:T(512)S(1)}, f32[512,2560]{1,0:T(8,128)S(1)}) fusion(bf16[2560,256]{1,0:T(8,128)(2,1)S(1)} %get-tuple-element.165, bf16[10,512,256]{1,2,0:T(8,128)(2,1)} %get-tuple-element.164, s32[]{:T(128)} %get-tuple-element.154, pred[2560]{0:T(1024)(128)(4,1)S(1)} %get-tuple-element.168, s32[512]{0:T(512)S(1)} %get-tuple-element.167), kind=kOutput, calls=%fused_computation.38.clone.1 | convolution fusion | flops 680263168 | bytes 6822912 | tf_op jit(solution)/shard_map/while/body/eval_jaxpr/dot_general | solution.py:35
  259.6 0.8 fusion.34
  260.5 0.5 copy-done.4
  260.9 2.0 fusion.35
  263.0 3.2 %fusion.33 = (f32[512]{0:T(512)S(1)}, f32[512,2560]{1,0:T(8,128)S(1)}) fusion(bf16[2560,256]{1,0:T(8,128)(2,1)S(1)} %get-tuple-element.165, bf16[10,512,256]{1,2,0:T(8,128)(2,1)} %get-tuple-element.164, s32[]{:T(128)} %get-tuple-element.154, pred[2560]{0:T(1024)(128)(4,1)S(1)} %get-tuple-element.168, s32[512]{0:T(512)S(1)} %get-tuple-element.167), kind=kOutput, calls=%fused_computation.38.clone.1 | convolution fusion | flops 680263168 | bytes 6822912 | tf_op jit(solution)/shard_map/while/body/eval_jaxpr/dot_general | solution.py:35
  266.2 0.8 fusion.34
  267.0 0.5 copy-done.4
  267.5 2.0 fusion.35
  269.5 3.2 %fusion.33 = (f32[512]{0:T(512)S(1)}, f32[512,2560]{1,0:T(8,128)S(1)}) fusion(bf16[2560,256]{1,0:T(8,128)(2,1)S(1)} %get-tuple-element.165, bf16[10,512,256]{1,2,0:T(8,128)(2,1)} %get-tuple-element.164, s32[]{:T(128)} %get-tuple-element.154, pred[2560]{0:T(1024)(128)(4,1)S(1)} %get-tuple-element.168, s32[512]{0:T(512)S(1)} %get-tuple-element.167), kind=kOutput, calls=%fused_computation.38.clone.1 | convolution fusion | flops 680263168 | bytes 6822912 | tf_op jit(solution)/shard_map/while/body/eval_jaxpr/dot_general | solution.py:35
  272.8 0.8 fusion.34
  273.6 0.5 copy-done.4
  274.1 2.0 fusion.35
  276.1 3.2 %fusion.33 = (f32[512]{0:T(512)S(1)}, f32[512,2560]{1,0:T(8,128)S(1)}) fusion(bf16[2560,256]{1,0:T(8,128)(2,1)S(1)} %get-tuple-element.165, bf16[10,512,256]{1,2,0:T(8,128)(2,1)} %get-tuple-element.164, s32[]{:T(128)} %get-tuple-element.154, pred[2560]{0:T(1024)(128)(4,1)S(1)} %get-tuple-element.168, s32[512]{0:T(512)S(1)} %get-tuple-element.167), kind=kOutput, calls=%fused_computation.38.clone.1 | convolution fusion | flops 680263168 | bytes 6822912 | tf_op jit(solution)/shard_map/while/body/eval_jaxpr/dot_general | solution.py:35
  279.4 0.8 fusion.34
  280.2 0.5 copy-done.4
  280.7 2.0 fusion.35
  282.7 3.2 %fusion.33 = (f32[512]{0:T(512)S(1)}, f32[512,2560]{1,0:T(8,128)S(1)}) fusion(bf16[2560,256]{1,0:T(8,128)(2,1)S(1)} %get-tuple-element.165, bf16[10,512,256]{1,2,0:T(8,128)(2,1)} %get-tuple-element.164, s32[]{:T(128)} %get-tuple-element.154, pred[2560]{0:T(1024)(128)(4,1)S(1)} %get-tuple-element.168, s32[512]{0:T(512)S(1)} %get-tuple-element.167), kind=kOutput, calls=%fused_computation.38.clone.1 | convolution fusion | flops 680263168 | bytes 6822912 | tf_op jit(solution)/shard_map/while/body/eval_jaxpr/dot_general | solution.py:35
  286.0 0.8 fusion.34
  286.8 0.5 copy-done.4
  287.3 2.0 fusion.35
  289.3 3.2 %fusion.33 = (f32[512]{0:T(512)S(1)}, f32[512,2560]{1,0:T(8,128)S(1)}) fusion(bf16[2560,256]{1,0:T(8,128)(2,1)S(1)} %get-tuple-element.165, bf16[10,512,256]{1,2,0:T(8,128)(2,1)} %get-tuple-element.164, s32[]{:T(128)} %get-tuple-element.154, pred[2560]{0:T(1024)(128)(4,1)S(1)} %get-tuple-element.168, s32[512]{0:T(512)S(1)} %get-tuple-element.167), kind=kOutput, calls=%fused_computation.38.clone.1 | convolution fusion | flops 680263168 | bytes 6822912 | tf_op jit(solution)/shard_map/while/body/eval_jaxpr/dot_general | solution.py:35
  292.6 0.8 fusion.34
  293.4 0.5 copy-done.4
  293.9 2.0 fusion.35
  295.9 3.2 %fusion.33 = (f32[512]{0:T(512)S(1)}, f32[512,2560]{1,0:T(8,128)S(1)}) fusion(bf16[2560,256]{1,0:T(8,128)(2,1)S(1)} %get-tuple-element.165, bf16[10,512,256]{1,2,0:T(8,128)(2,1)} %get-tuple-element.164, s32[]{:T(128)} %get-tuple-element.154, pred[2560]{0:T(1024)(128)(4,1)S(1)} %get-tuple-element.168, s32[512]{0:T(512)S(1)} %get-tuple-element.167), kind=kOutput, calls=%fused_computation.38.clone.1 | convolution fusion | flops 680263168 | bytes 6822912 | tf_op jit(solution)/shard_map/while/body/eval_jaxpr/dot_general | solution.py:35
  299.2 0.8 fusion.34
  300.0 0.5 copy-done.4
  300.5 2.0 fusion.35
  302.5 2.2 fusion.14
  304.7 2.8 copy.23
  (33 shorter events, 0.2 us)
Async XLA Ops:
  6.5 136.4 %copy-start.3 = (bf16[512,2560]{1,0:T(8,128)(2,1)S(1)}, bf16[512,2560]{1,0:T(8,128)(2,1)}, u32[]{:S(2)}) copy-start(bf16[512,2560]{1,0:T(8,128)(2,1)} %param.9) | copy-start | bytes 7864324
  6.5 136.4 %copy-start.5 = (f32[2560]{0:T(1024)S(1)}, f32[2560]{0:T(1024)}, u32[]{:S(2)}) copy-start(f32[2560]{0:T(1024)} %param.10) | copy-start | bytes 30724
  6.5 28.3 %all-gather.7.cloned.1.call-start = ((), (), s32[]{:S(2)}) async-start(), calls=%async_computation.3 | async-start | bytes 1179648 | tf_op jit(solution)/shard_map/all_gather | solution.py:62
  7.3 135.7 %all-gather.5.cloned.1.call-start = ((), (), s32[]{:S(2)}) async-start(), calls=%async_computation.2 | async-start | bytes 16711680 | tf_op jit(solution)/shard_map/all_gather | solution.py:52
  10.6 145.4 %all-to-all-start = ((s32[16,32,1]{1,2,0:T(1,128)}), s32[16,32,1]{1,2,0:T(1,128)S(1)}, u32[]{:S(2)}, u32[]{:S(2)}) async-start(s32[16,32,1]{1,2,0:T(1,128)} %all_to_all.14), calls=%async_computation | async-start | bytes 16384 | tf_op jit(solution)/shard_map/all_to_all | solution.py:57
  18.6 196.7 %all-gather.9.cloned.1.call-start = ((), (), s32[]{:S(2)}) async-start(), calls=%async_computation.4 | async-start | bytes 2228224 | tf_op jit(solution)/shard_map/all_gather | solution.py:64
  156.0 62.3 %all-to-all-start.1 = ((bf16[16,32,3072]{2,1,0:T(8,128)(2,1)}), bf16[16,32,3072]{2,1,0:T(8,128)(2,1)S(1)}, u32[]{:S(2)}, u32[]{:S(2)}) async-start(bf16[16,32,3072]{2,1,0:T(8,128)(2,1)} %bitcast.2), calls=%async_computation.1 | async-start | bytes 6291456 | tf_op jit(solution)/shard_map/all_to_all | solution.py:56
  218.3 1.6 copy-start.2
  229.8 4.5 %copy-start = (bf16[2048,256]{1,0:T(8,128)(2,1)S(1)}, bf16[2048,256]{1,0:T(8,128)(2,1)}, u32[]{:S(2)}) copy-start(bf16[2048,256]{1,0:T(8,128)(2,1)} %get-tuple-element.93) | copy-start | bytes 3145732
  229.8 4.5 %copy-start.1 = (bf16[2048,256]{1,0:T(8,128)(2,1)S(1)}, bf16[2048,256]{1,0:T(8,128)(2,1)}, u32[]{:S(2)}) copy-start(bf16[2048,256]{1,0:T(8,128)(2,1)} %get-tuple-element.94) | copy-start | bytes 3145732
  239.8 1.3 copy-start.4
  246.4 1.3 copy-start.4
  253.0 1.3 copy-start.4
  259.6 1.3 copy-start.4
  266.2 1.3 copy-start.4
  272.8 1.3 copy-start.4
  279.4 1.3 copy-start.4
  286.0 1.3 copy-start.4
  292.6 1.3 copy-start.4
  299.2 1.3 copy-start.4
Sparse Core Ops, SparseCore 0:
  9.0 25.7 all-gather.6
  37.0 105.9 all-gather.4
  145.1 70.1 all-gather.8
where the time goes:
time: 316 us; the launch traced here: 314 us
  waiting for transfers between devices  174 us (55%)
  matrix products  65.7 us (21%)
  local copies, waits for them, and re-layouts  29.4 us (9%)
  other arithmetic  16.6 us (5%)
  between operations  14.5 us (5%)
  starting transfers between devices  13.3 us (4%)
    all_gather x1, waiting for transfers between devices, shards(): lax.all_gather(w_qkv, 'shard', axis=1, tiled=True)  107 us
    all_gather x1, waiting for transfers between devices, shards(): prefix = lax.all_gather(chosen, 'shard', axis=0, tiled=True)  53.2 us
    dot_general x10, matrix products, one_head(): jnp.dot(head_q, keys.T, preferred_element_type=jnp.float32) * HD ** (-0.5)  32.4 us
    dot_general x10, matrix products, one_head(): return jnp.dot(weights, values, preferred_element_type=jnp.float32)  20.2 us
    all_gather x1, waiting for transfers between devices, shards(): sliced = lax.all_gather(prefix_kv, 'grp', axis=0, tiled=True)  13.2 us
    dot_general x1, matrix products, shards(): jnp.dot(normed, lax.all_gather(w_qkv, 'shard', axis=1, tiled=True), prefe...  13 us
    reduce_sum x10, other arithmetic, one_head(): jnp.sum(expd, axis=-1, keepdims=True)  8.39 us
    all_to_all x1, starting transfers between devices, shards(): lax.all_to_all(order, 'shard', split_axis=0, concat_axis=0, tiled=True)  7.99 us
  transfers between devices with their start and end apart: 5, of which 3 were waited for; matrix products, arithmetic and copies ran while one was open for 7% of the time, Pallas kernels for 0%

commit v1 on v0

--- a/solution.py
+++ b/solution.py
@@ -43,29 +43,52 @@
     return jnp.where(query_pos < length, result, 0.0).astype(jnp.bfloat16)
 
 
+def gather_by_a2a(piece, axis_name, count):
+    spread = jnp.broadcast_to(piece[None], (count,) + piece.shape)
+    return lax.all_to_all(spread, axis_name, 0, 0, tiled=True)
+
+
 def shards(tokens, gain, w_qkv, prefix_kv, prefix_owner, suffix_len, slots):
     tok_dev = tokens.shape[0]
+    n_grp = lax.axis_size("grp")
+    n_shard = lax.axis_size("shard")
+    grp = lax.axis_index("grp")
+    core = grp % 2
+    pairs = [(g, g ^ 1) for g in range(n_grp)]
+
+    normed = normalize(tokens, gain)
+    partner_rows = lax.ppermute(normed, "grp", pairs)
+
+    cols = w_qkv.shape[1]
+    half = cols // 2
+    w_mine = lax.dynamic_slice_in_dim(w_qkv, core * half, half, axis=1)
+    w_gathered = lax.all_gather(w_mine, "shard", axis=1, tiled=True)
+    both = jnp.concatenate([normed, partner_rows], axis=0)
+    out = jnp.dot(both, w_gathered, preferred_element_type=jnp.float32).astype(jnp.bfloat16)
+    out_mine = out[:tok_dev]
+    out_back = lax.ppermute(out[tok_dev:], "grp", pairs)
+    is0 = core == 0
+    half0 = jnp.where(is0, out_mine, out_back).reshape(tok_dev, n_shard, 1, half)
+    half1 = jnp.where(is0, out_back, out_mine).reshape(tok_dev, n_shard, 1, half)
+    projected = jnp.concatenate([half0, half1], axis=2).reshape(tok_dev, n_shard * cols)
+
     order = slots.reshape(tok_dev)
-    normed = normalize(tokens, gain)
-    projected = jnp.dot(
-        normed,
-        lax.all_gather(w_qkv, "shard", axis=1, tiled=True),
-        preferred_element_type=jnp.float32,
-    ).astype(jnp.bfloat16)
     arrived, order = (
         lax.all_to_all(projected, "shard", split_axis=0, concat_axis=0, tiled=True),
         lax.all_to_all(order, "shard", split_axis=0, concat_axis=0, tiled=True),
     )
     first_slot = lax.axis_index("shard") * tok_dev
-    placed = jnp.zeros_like(arrived).at[order - first_slot].set(arrived)
+    pos = order - first_slot
+    onehot = (jnp.arange(tok_dev, dtype=jnp.int32)[:, None] == pos[None, :]).astype(jnp.bfloat16)
+    placed = jnp.dot(onehot, arrived, preferred_element_type=jnp.float32).astype(jnp.bfloat16)
+
     owner = prefix_owner[0]
-    sliced = lax.all_gather(prefix_kv, "grp", axis=0, tiled=True)
+    sliced = gather_by_a2a(prefix_kv[0], "grp", n_grp)
     chosen = lax.dynamic_index_in_dim(sliced, owner, 0, keepdims=False)
-    prefix = lax.all_gather(chosen, "shard", axis=0, tiled=True)
+    prefix = gather_by_a2a(chosen, "shard", n_shard).reshape(-1, chosen.shape[-1])
+
     lengths = suffix_len.reshape(-1)
-    req_count = lengths.shape[0]
-    blocks = placed.reshape(req_count, SUF, placed.shape[1])
-    results = attend_request(blocks[0, :, :HQ], blocks[0, :, HQ:], prefix, lengths[0])
+    results = attend_request(placed[:, :HQ], placed[:, HQ:], prefix, lengths[0])
     return results
 
 

time: 316 us -> 303 us (0.959)
  waiting for transfers between devices: 174 us -> 111 us
  local copies, waits for them, and re-layouts: 29.4 us -> 54.7 us
  other arithmetic: 16.6 us -> 26.8 us
  starting transfers between devices: 13.3 us -> 20.9 us
  matrix products: 65.7 us -> 73.1 us
    all_gather x3 -> x1, waiting for transfers between devices: 173 us -> 61.6 us  [shards(): w_gathered = lax.all_gather(w_mine, 'shard', axis=1, tiled=True)]
    all_to_all x1, waiting for transfers between devices: 0.01 us -> 42.2 us  [shards(): lax.all_to_all(projected, 'shard', split_axis=0, concat_axis=0, tiled=True)]
    all_to_all x0 -> x1, local copies, waits for them, and re-layouts: none -> 12.4 us  [shards(): lax.all_to_all(projected, 'shard', split_axis=0, concat_axis=0, tiled=True)]
    concatenate x0 -> x1, local copies, waits for them, and re-layouts: none -> 11.2 us  [shards(): jnp.concatenate([half0, half1], axis=2).reshape(tok_dev, n_shard * cols)]
    all_to_all x0 -> x2, starting transfers between devices: none -> 8.41 us  [gather_by_a2a(): return lax.all_to_all(spread, axis_name, 0, 0, tiled=True)]
    all_to_all x1, waiting for transfers between devices: 0.01 us -> 7.48 us  [shards(): lax.all_to_all(order, 'shard', split_axis=0, concat_axis=0, tiled=True)]
    scatter x1 -> x0, local copies, waits for them, and re-layouts: 7.31 us -> none  [shards(): placed = jnp.zeros_like(arrived).at[order - first_slot].set(arrived)]
    select_n x0 -> x2, local copies, waits for them, and re-layouts: none -> 5.23 us  [the longest x1 2.63 us: shards(): jnp.where(is0, out_mine, out_back).reshape(tok_dev, n_shard, 1, half)]
  transfers between devices with their start and end apart: 5 -> 7, of which waited for: 3 -> 3; matrix products, arithmetic and copies ran while one was open for 7% -> 16% of each run, Pallas kernels for 0% -> 0%
where the time goes in v1:
time: 303 us; the launch traced here: 302 us
  waiting for transfers between devices  111 us (37%)
  matrix products  73.1 us (24%)
  local copies, waits for them, and re-layouts  54.7 us (18%)
  other arithmetic  26.8 us (9%)
  starting transfers between devices  20.9 us (7%)
  between operations  14.9 us (5%)
    all_gather x1, waiting for transfers between devices, shards(): w_gathered = lax.all_gather(w_mine, 'shard', axis=1, tiled=True)  61.6 us
    all_to_all x1, waiting for transfers between devices, shards(): lax.all_to_all(projected, 'shard', split_axis=0, concat_axis=0, tiled=True)  42.2 us
    dot_general x10, matrix products, one_head(): jnp.dot(head_q, keys.T, preferred_element_type=jnp.float32) * HD ** (-0.5)  37 us
    dot_general x10, matrix products, one_head(): return jnp.dot(weights, values, preferred_element_type=jnp.float32)  20.2 us
    all_to_all x1, local copies, waits for them, and re-layouts, shards(): lax.all_to_all(projected, 'shard', split_axis=0, concat_axis=0, tiled=True)  12.4 us
    dot_general x1, matrix products, shards(): jnp.dot(both, w_gathered, preferred_element_type=jnp.float32)  12.2 us
    concatenate x1, local copies, waits for them, and re-layouts, shards(): jnp.concatenate([half0, half1], axis=2).reshape(tok_dev, n_shard * cols)  11.2 us
    all_to_all x2, starting transfers between devices, gather_by_a2a(): return lax.all_to_all(spread, axis_name, 0, 0, tiled=True)  8.41 us
  transfers between devices with their start and end apart: 7, of which 3 were waited for; matrix products, arithmetic and copies ran while one was open for 16% of the time, Pallas kernels for 0%

profile of v1, /device:TPU:0, one launch (start us, length us, event | category | flops | bytes accessed | tf_op | source)
XLA Modules:
  0.0 301.8 jit_solution(2866371976029989938)
XLA Ops:
  6.5 1.2 copy-done
  7.7 0.8 constant_dynamic-slice_fusion
  8.6 2.5 fusion.11
  11.1 2.2 fusion.13
  13.3 1.1 broadcast_in_dim.49
  14.3 4.7 %all-to-all-start.2 = ((bf16[8,128,512]{2,1,0:T(8,128)(2,1)}), bf16[8,128,512]{2,1,0:T(8,128)(2,1)S(1)}, u32[]{:S(2)}, u32[]{:S(2)}) async-start(bf16[8,128,512]{2,1,0:T(8,128)(2,1)} %broadcast_in_dim.49), calls=%async_computation.2 | async-start | bytes 2097152 | tf_op jit(solution)/shard_map/all_to_all | solution.py:48
  19.0 61.6 %all-gather.2.cloned.1.call-done = bf16[2560,1536]{0,1:T(8,128)(2,1)} async-done(((bf16[2560,96]{0,1:T(8,128)(2,1)}), bf16[2560,1536]{0,1:T(8,128)(2,1)}) %all-gather.2.cloned.1.call-update) | async-done | bytes 7864336 | tf_op jit(solution)/shard_map/all_gather | solution.py:65
  80.6 12.2 %fusion.19 = bf16[1024,1536]{1,0:T(8,128)(2,1)S(1)} fusion(bf16[2560,1536]{0,1:T(8,128)(2,1)} %all-gather.2.cloned.1.call-done, bf16[512,2560]{1,0:T(8,128)(2,1)} %collective-permute-done, bf16[512,2560]{1,0:T(8,128)(2,1)} %fusion.13), kind=kOutput, calls=%fused_computation.27 | convolution fusion | flops 8065122304 | bytes 16252928 | tf_op jit(solution)/shard_map/dot_general | solution.py:67
  92.9 1.6 copy-done.5
  94.5 1.3 slice.32
  95.8 0.5 broadcast.60
  96.3 0.7 reduce.7
  97.0 0.7 all_to_all.20
  98.3 5.3 %all-to-all-start = ((s32[16,32,1]{1,2,0:T(1,128)}), s32[16,32,1]{1,2,0:T(1,128)S(1)}, u32[]{:S(2)}, u32[]{:S(2)}) async-start(s32[16,32,1]{1,2,0:T(1,128)} %all_to_all.20), calls=%async_computation | async-start | bytes 16384 | tf_op jit(solution)/shard_map/all_to_all | solution.py:78
  103.6 7.5 %all-to-all-done = s32[16,32,1]{1,2,0:T(1,128)S(1)} async-done(((s32[16,32,1]{1,2,0:T(1,128)}), s32[16,32,1]{1,2,0:T(1,128)S(1)}, u32[]{:S(2)}, u32[]{:S(2)}) %all-to-all-start) | async-done | bytes 2080 | tf_op jit(solution)/shard_map/all_to_all | solution.py:78
  111.1 1.5 broadcast_in_dim.51
  112.6 3.7 %all-to-all-start.3 = ((bf16[16,128,512]{2,1,0:T(8,128)(2,1)}), bf16[16,128,512]{2,1,0:T(8,128)(2,1)S(1)}, u32[]{:S(2)}, u32[]{:S(2)}) async-start(bf16[16,128,512]{2,1,0:T(8,128)(2,1)} %broadcast_in_dim.51), calls=%async_computation.3 | async-start | bytes 4194304 | tf_op jit(solution)/shard_map/all_to_all | solution.py:48
  116.4 3.8 %broadcast_select_fusion.1 = (bf16[512,1536]{1,0:T(8,128)(2,1)}, bf16[512,1536]{1,0:T(8,128)(2,1)}) fusion(bf16[512,1536]{1,0:T(8,128)(2,1)} %collective-permute-done.1, pred[]{:T(512)S(6)} %eq.21, bf16[1024,1536]{1,0:T(8,128)(2,1)} %copy-done.5), kind=kLoop, calls=%fused_computation.30 | loop fusion | flops 1572864 | bytes 6291457 | tf_op jit(solution)/shard_map/jit(_where)/select_n | solution.py:71
  120.1 2.6 copy.17
  122.7 2.6 copy.18
  125.3 3.9 %pad_maximum_fusion = bf16[512,16,2,96]{0,3,1,2:T(8,128)(2,1)} fusion(bf16[512,16,1,96]{0,3,1,2:T(8,128)(2,1)} %bitcast.48, bf16[512,16,1,96]{0,3,1,2:T(8,128)(2,1)} %bitcast.47), kind=kLoop, calls=%fused_computation.28 | loop fusion | flops 1572864 | bytes 6291456 | tf_op jit(solution)/shard_map/concatenate | solution.py:73
  129.2 11.2 %copy.19 = bf16[512,16,2,96]{3,2,1,0:T(2,128)(2,1)} copy(bf16[512,16,2,96]{0,3,1,2:T(8,128)(2,1)} %pad_maximum_fusion) | data formatting | bytes 6291456 | tf_op jit(solution)/shard_map/concatenate | solution.py:73
  140.4 12.4 %all_to_all.22 = bf16[16,32,3072]{2,1,0:T(8,128)(2,1)} reshape(bf16[512,16,2,96]{3,2,1,0:T(2,128)(2,1)} %copy.19) | data formatting | bytes 6291456 | tf_op jit(solution)/shard_map/all_to_all | solution.py:77
  152.8 7.2 %all-to-all-start.1 = ((bf16[16,32,3072]{2,1,0:T(8,128)(2,1)}), bf16[16,32,3072]{2,1,0:T(8,128)(2,1)}, u32[]{:S(2)}, u32[]{:S(2)}) async-start(bf16[16,32,3072]{2,1,0:T(8,128)(2,1)} %all_to_all.22), calls=%async_computation.1 | async-start | bytes 6291456 | tf_op jit(solution)/shard_map/all_to_all | solution.py:77
  160.8 1.5 fusion.26
  162.4 42.2 %all-to-all-done.1 = bf16[16,32,3072]{2,1,0:T(8,128)(2,1)} async-done(((bf16[16,32,3072]{2,1,0:T(8,128)(2,1)}), bf16[16,32,3072]{2,1,0:T(8,128)(2,1)}, u32[]{:S(2)}, u32[]{:S(2)}) %all-to-all-start.1) | async-done | bytes 3145760 | tf_op jit(solution)/shard_map/all_to_all | solution.py:77
  204.6 3.7 %convolution_convert_fusion = bf16[512,3072]{1,0:T(8,128)(2,1)S(1)} fusion(bf16[512,3072]{1,0:T(8,128)(2,1)} %bitcast.3, s32[512]{0:T(512)S(1)} %sub.24), kind=kOutput, calls=%fused_computation.26 | convolution fusion | flops 1612447744 | bytes 6293504 | tf_op jit(solution)/shard_map/dot_general | solution.py:83
  208.3 1.7 slice.33
  210.0 4.6 %copy.20 = bf16[512,2560]{0,1:T(8,128)(2,1)} copy(bf16[512,2560]{1,0:T(8,128)(2,1)} %slice.33) | data formatting | bytes 5242880 | tf_op jit(solution)/shard_map/slice | solution.py:91
  214.6 1.7 pad_maximum_fusion.1
  216.3 70.5 %while.11 = (s32[]{:T(128)}, bf16[10,512,256]{1,2,0:T(8,128)(2,1)}, bf16[10,512,256]{1,2,0:T(8,128)(2,1)}, bf16[2560,256]{1,0:T(8,128)(2,1)}, bf16[2560,256]{1,0...) while((s32[]{:T(128)}, bf16[10,512,256]{1,2,0:T(8,128)(2,1)}, ...), condition=%wide.region_4.5_spmd.clone, body=%wide.region_1.4_spmd.clone.sunk | while | flops 1357904896 | bytes 24395376 | solution.py:42
  216.3 3.7 %fusion.38 = (f32[512]{0:T(512)S(1)}, f32[512,2560]{1,0:T(8,128)S(1)}) fusion(bf16[2560,256]{1,0:T(8,128)(2,1)} %get-tuple-element.160, bf16[10,512,256]{1,2,0:T(8,128)(2,1)} %get-tuple-element.159, s32[]{:T(128)} %get-tuple-element.149, pred[2560]{0:T(1024)(128)(4,1)S(1)} %get-tuple-element.163, s32[512]{0:T(512)S(1)} %get-tuple-element.162), kind=kOutput, calls=%fused_computation.43.clone.1 | convolution fusion | flops 680263168 | bytes 6822912 | tf_op jit(solution)/shard_map/while/body/eval_jaxpr/dot_general | solution.py:35
  220.0 0.8 fusion.39
  221.3 2.0 fusion.40
  223.3 3.7 %fusion.38 = (f32[512]{0:T(512)S(1)}, f32[512,2560]{1,0:T(8,128)S(1)}) fusion(bf16[2560,256]{1,0:T(8,128)(2,1)} %get-tuple-element.160, bf16[10,512,256]{1,2,0:T(8,128)(2,1)} %get-tuple-element.159, s32[]{:T(128)} %get-tuple-element.149, pred[2560]{0:T(1024)(128)(4,1)S(1)} %get-tuple-element.163, s32[512]{0:T(512)S(1)} %get-tuple-element.162), kind=kOutput, calls=%fused_computation.43.clone.1 | convolution fusion | flops 680263168 | bytes 6822912 | tf_op jit(solution)/shard_map/while/body/eval_jaxpr/dot_general | solution.py:35
  227.0 0.8 fusion.39
  228.3 2.0 fusion.40
  230.4 3.7 %fusion.38 = (f32[512]{0:T(512)S(1)}, f32[512,2560]{1,0:T(8,128)S(1)}) fusion(bf16[2560,256]{1,0:T(8,128)(2,1)} %get-tuple-element.160, bf16[10,512,256]{1,2,0:T(8,128)(2,1)} %get-tuple-element.159, s32[]{:T(128)} %get-tuple-element.149, pred[2560]{0:T(1024)(128)(4,1)S(1)} %get-tuple-element.163, s32[512]{0:T(512)S(1)} %get-tuple-element.162), kind=kOutput, calls=%fused_computation.43.clone.1 | convolution fusion | flops 680263168 | bytes 6822912 | tf_op jit(solution)/shard_map/while/body/eval_jaxpr/dot_general | solution.py:35
  234.1 0.8 fusion.39
  234.9 0.5 copy-done.6
  235.4 2.0 fusion.40
  237.4 3.7 %fusion.38 = (f32[512]{0:T(512)S(1)}, f32[512,2560]{1,0:T(8,128)S(1)}) fusion(bf16[2560,256]{1,0:T(8,128)(2,1)} %get-tuple-element.160, bf16[10,512,256]{1,2,0:T(8,128)(2,1)} %get-tuple-element.159, s32[]{:T(128)} %get-tuple-element.149, pred[2560]{0:T(1024)(128)(4,1)S(1)} %get-tuple-element.163, s32[512]{0:T(512)S(1)} %get-tuple-element.162), kind=kOutput, calls=%fused_computation.43.clone.1 | convolution fusion | flops 680263168 | bytes 6822912 | tf_op jit(solution)/shard_map/while/body/eval_jaxpr/dot_general | solution.py:35
  241.1 0.8 fusion.39
  242.4 2.0 fusion.40
  244.5 3.7 %fusion.38 = (f32[512]{0:T(512)S(1)}, f32[512,2560]{1,0:T(8,128)S(1)}) fusion(bf16[2560,256]{1,0:T(8,128)(2,1)} %get-tuple-element.160, bf16[10,512,256]{1,2,0:T(8,128)(2,1)} %get-tuple-element.159, s32[]{:T(128)} %get-tuple-element.149, pred[2560]{0:T(1024)(128)(4,1)S(1)} %get-tuple-element.163, s32[512]{0:T(512)S(1)} %get-tuple-element.162), kind=kOutput, calls=%fused_computation.43.clone.1 | convolution fusion | flops 680263168 | bytes 6822912 | tf_op jit(solution)/shard_map/while/body/eval_jaxpr/dot_general | solution.py:35
  248.2 0.8 fusion.39
  249.5 2.0 fusion.40
  251.5 3.7 %fusion.38 = (f32[512]{0:T(512)S(1)}, f32[512,2560]{1,0:T(8,128)S(1)}) fusion(bf16[2560,256]{1,0:T(8,128)(2,1)} %get-tuple-element.160, bf16[10,512,256]{1,2,0:T(8,128)(2,1)} %get-tuple-element.159, s32[]{:T(128)} %get-tuple-element.149, pred[2560]{0:T(1024)(128)(4,1)S(1)} %get-tuple-element.163, s32[512]{0:T(512)S(1)} %get-tuple-element.162), kind=kOutput, calls=%fused_computation.43.clone.1 | convolution fusion | flops 680263168 | bytes 6822912 | tf_op jit(solution)/shard_map/while/body/eval_jaxpr/dot_general | solution.py:35
  255.2 0.8 fusion.39
  256.5 2.0 fusion.40
  258.5 3.7 %fusion.38 = (f32[512]{0:T(512)S(1)}, f32[512,2560]{1,0:T(8,128)S(1)}) fusion(bf16[2560,256]{1,0:T(8,128)(2,1)} %get-tuple-element.160, bf16[10,512,256]{1,2,0:T(8,128)(2,1)} %get-tuple-element.159, s32[]{:T(128)} %get-tuple-element.149, pred[2560]{0:T(1024)(128)(4,1)S(1)} %get-tuple-element.163, s32[512]{0:T(512)S(1)} %get-tuple-element.162), kind=kOutput, calls=%fused_computation.43.clone.1 | convolution fusion | flops 680263168 | bytes 6822912 | tf_op jit(solution)/shard_map/while/body/eval_jaxpr/dot_general | solution.py:35
  262.3 0.8 fusion.39
  263.6 2.0 fusion.40
  265.6 3.7 %fusion.38 = (f32[512]{0:T(512)S(1)}, f32[512,2560]{1,0:T(8,128)S(1)}) fusion(bf16[2560,256]{1,0:T(8,128)(2,1)} %get-tuple-element.160, bf16[10,512,256]{1,2,0:T(8,128)(2,1)} %get-tuple-element.159, s32[]{:T(128)} %get-tuple-element.149, pred[2560]{0:T(1024)(128)(4,1)S(1)} %get-tuple-element.163, s32[512]{0:T(512)S(1)} %get-tuple-element.162), kind=kOutput, calls=%fused_computation.43.clone.1 | convolution fusion | flops 680263168 | bytes 6822912 | tf_op jit(solution)/shard_map/while/body/eval_jaxpr/dot_general | solution.py:35
  269.3 0.8 fusion.39
  270.6 2.0 fusion.40
  272.6 3.7 %fusion.38 = (f32[512]{0:T(512)S(1)}, f32[512,2560]{1,0:T(8,128)S(1)}) fusion(bf16[2560,256]{1,0:T(8,128)(2,1)} %get-tuple-element.160, bf16[10,512,256]{1,2,0:T(8,128)(2,1)} %get-tuple-element.159, s32[]{:T(128)} %get-tuple-element.149, pred[2560]{0:T(1024)(128)(4,1)S(1)} %get-tuple-element.163, s32[512]{0:T(512)S(1)} %get-tuple-element.162), kind=kOutput, calls=%fused_computation.43.clone.1 | convolution fusion | flops 680263168 | bytes 6822912 | tf_op jit(solution)/shard_map/while/body/eval_jaxpr/dot_general | solution.py:35
  276.4 0.8 fusion.39
  277.7 2.0 fusion.40
  279.7 3.7 %fusion.38 = (f32[512]{0:T(512)S(1)}, f32[512,2560]{1,0:T(8,128)S(1)}) fusion(bf16[2560,256]{1,0:T(8,128)(2,1)} %get-tuple-element.160, bf16[10,512,256]{1,2,0:T(8,128)(2,1)} %get-tuple-element.159, s32[]{:T(128)} %get-tuple-element.149, pred[2560]{0:T(1024)(128)(4,1)S(1)} %get-tuple-element.163, s32[512]{0:T(512)S(1)} %get-tuple-element.162), kind=kOutput, calls=%fused_computation.43.clone.1 | convolution fusion | flops 680263168 | bytes 6822912 | tf_op jit(solution)/shard_map/while/body/eval_jaxpr/dot_general | solution.py:35
  283.4 0.8 fusion.39
  284.7 2.0 fusion.40
  286.7 3.8 %fusion.18 = bf16[512,2560]{0,1:T(8,128)(2,1)} fusion(bf16[10,512,256]{1,2,0:T(8,128)(2,1)} %get-tuple-element.37, pred[512]{0:T(512)(128)(4,1)S(1)} %iota_compare_fusion.5), kind=kLoop, calls=%fused_computation.25 | loop fusion | flops 1310720 | bytes 5243392 | tf_op jit(solution)/shard_map/convert_element_type | solution.py:43
  290.5 4.4 %copy.23 = bf16[512,2560]{1,0:T(8,128)(2,1)} copy(bf16[512,2560]{0,1:T(8,128)(2,1)} %fusion.18) | data formatting | bytes 5242880 | tf_op jit(solution)/shard_map/convert_element_type | solution.py:43
  (52 shorter events, 4.6 us)
Async XLA Ops:
  6.5 1.2 copy-start
  6.5 4.5 %copy-start.8 = (f32[2560]{0:T(1024)S(1)}, f32[2560]{0:T(1024)}, u32[]{:S(2)}) copy-start(f32[2560]{0:T(1024)} %param.10) | copy-start | bytes 30724
  6.5 74.1 %all-gather.2.cloned.1.call-start = ((), (), s32[]{:S(2)}) async-start(), calls=%async_computation.4 | async-start | bytes 8355840 | tf_op jit(solution)/shard_map/all_gather | solution.py:65
  8.6 2.5 copy-start.2
  11.1 2.2 copy-start.7
  13.3 5.8 %collective-permute-start = (bf16[512,2560]{1,0:T(8,128)(2,1)}, bf16[512,2560]{1,0:T(8,128)(2,1)}, u32[]{:S(2)}, u32[]{:S(2)}) collective-permute-start(bf16[512,2560]{1,0:T(8,128)(2,1)} %fusion.13), channel_id=1, source_target_pairs={{0,16},{16,0},{32,48},{48,32},{64,80},{80,64},{96,112},{112,96},{1... | collective-permute-start | bytes 7864328 | tf_op jit(solution)/shard_map/ppermute | solution.py:60
  14.3 84.0 %all-to-all-start.2 = ((bf16[8,128,512]{2,1,0:T(8,128)(2,1)}), bf16[8,128,512]{2,1,0:T(8,128)(2,1)S(1)}, u32[]{:S(2)}, u32[]{:S(2)}) async-start(bf16[8,128,512]{2,1,0:T(8,128)(2,1)} %broadcast_in_dim.49), calls=%async_computation.2 | async-start | bytes 2097152 | tf_op jit(solution)/shard_map/all_to_all | solution.py:48
  92.9 1.6 copy-start.5
  94.5 1.8 copy-start.9
  95.8 20.6 %collective-permute-start.1 = (bf16[512,1536]{1,0:T(8,128)(2,1)}, bf16[512,1536]{1,0:T(8,128)(2,1)}, u32[]{:S(2)}, u32[]{:S(2)}) collective-permute-start(bf16[512,1536]{1,0:T(8,128)(2,1)} %slice.32), channel_id=1, source_target_pairs={{0,16},{16,0},{32,48},{48,32},{64,80},{80,64},{96,112},{112,96},{1... | collective-permute-start | bytes 4718600 | tf_op jit(solution)/shard_map/ppermute | solution.py:69
  98.3 12.8 %all-to-all-start = ((s32[16,32,1]{1,2,0:T(1,128)}), s32[16,32,1]{1,2,0:T(1,128)S(1)}, u32[]{:S(2)}, u32[]{:S(2)}) async-start(s32[16,32,1]{1,2,0:T(1,128)} %all_to_all.20), calls=%async_computation | async-start | bytes 16384 | tf_op jit(solution)/shard_map/all_to_all | solution.py:78
  112.6 40.2 %all-to-all-start.3 = ((bf16[16,128,512]{2,1,0:T(8,128)(2,1)}), bf16[16,128,512]{2,1,0:T(8,128)(2,1)S(1)}, u32[]{:S(2)}, u32[]{:S(2)}) async-start(bf16[16,128,512]{2,1,0:T(8,128)(2,1)} %broadcast_in_dim.51), calls=%async_computation.3 | async-start | bytes 4194304 | tf_op jit(solution)/shard_map/all_to_all | solution.py:48
  152.8 51.8 %all-to-all-start.1 = ((bf16[16,32,3072]{2,1,0:T(8,128)(2,1)}), bf16[16,32,3072]{2,1,0:T(8,128)(2,1)}, u32[]{:S(2)}, u32[]{:S(2)}) async-start(bf16[16,32,3072]{2,1,0:T(8,128)(2,1)} %all_to_all.22), calls=%async_computation.1 | async-start | bytes 6291456 | tf_op jit(solution)/shard_map/all_to_all | solution.py:77
  210.0 4.6 %copy-start.3 = (bf16[2048,256]{1,0:T(8,128)(2,1)S(1)}, bf16[2048,256]{1,0:T(8,128)(2,1)}, u32[]{:S(2)}) copy-start(bf16[2048,256]{1,0:T(8,128)(2,1)} %get-tuple-element.90) | copy-start | bytes 3145732
  210.0 4.6 %copy-start.4 = (bf16[2048,256]{1,0:T(8,128)(2,1)S(1)}, bf16[2048,256]{1,0:T(8,128)(2,1)}, u32[]{:S(2)}) copy-start(bf16[2048,256]{1,0:T(8,128)(2,1)} %get-tuple-element.91) | copy-start | bytes 3145732
  220.0 1.3 copy-start.6
  227.0 1.3 copy-start.6
  234.1 1.3 copy-start.6
  241.1 1.3 copy-start.6
  248.2 1.3 copy-start.6
  255.2 1.3 copy-start.6
  262.2 1.3 copy-start.6
  269.3 1.3 copy-start.6
  276.3 1.3 copy-start.6
  283.4 1.3 copy-start.6
  286.7 8.2 %copy-start.1 = (bf16[2560,192]{0,1:T(8,128)(2,1)S(1)}, bf16[2560,192]{0,1:T(8,128)(2,1)}, u32[]{:S(2)}) copy-start(bf16[2560,192]{0,1:T(8,128)(2,1)} %param.11) | copy-start | bytes 2949124
Sparse Core Ops, SparseCore 0:
  9.5 71.1 all-gather.1

commit v2 on v1

v2 whole, which is shorter than its diff:
```python
import jax
import jax.numpy as jnp
from jax import lax
from jax.experimental import pallas as pl
from jax.experimental.pallas import tpu as pltpu
from jax.sharding import PartitionSpec as P

H = 10
HD = 256
WINDOW = 2048
SUF = 512
HQ = 2560
TQ = 128


def normalize(rows, gain):
    rows32 = rows.astype(jnp.float32)
    factor = lax.rsqrt(jnp.mean(rows32 * rows32, axis=-1, keepdims=True) + 1e-06)
    return (rows32 * factor * gain).astype(jnp.bfloat16)


def _attn_kernel(len_ref, q_ref, pk_ref, pv_ref, sk_ref, sv_ref, o_ref):
    n = len_ref[0]
    pre = pk_ref.shape[0]
    count = q_ref.shape[0]
    scale = HD ** (-0.5)
    nt = (((1,), (1,)), ((), ()))
    for i in range(count // TQ):
        r0 = i * TQ
        q = q_ref[r0:r0 + TQ, :]
        qpos = r0 + lax.broadcasted_iota(jnp.int32, (TQ, 1), 0)
        sp = lax.dot_general(q, pk_ref[r0:, :], nt, preferred_element_type=jnp.float32) * scale
        ppos = r0 + lax.broadcasted_iota(jnp.int32, (1, pre - r0), 1)
        vis_p = (ppos > pre + qpos - WINDOW) & (ppos <= pre + qpos) & (ppos < pre + n)
        sp = jnp.where(vis_p, sp, -1e30)
        ns = r0 + TQ
        ss = lax.dot_general(q, sk_ref[:ns, :], nt, preferred_element_type=jnp.float32) * scale
        spos = pre + lax.broadcasted_iota(jnp.int32, (1, ns), 1)
        vis_s = (spos > pre + qpos - WINDOW) & (spos <= pre + qpos) & (spos < pre + n)
        ss = jnp.where(vis_s, ss, -1e30)
        top = jnp.maximum(jnp.max(sp, axis=-1, keepdims=True), jnp.max(ss, axis=-1, keepdims=True))
        ep = jnp.exp(sp - top)
        es = jnp.exp(ss - top)
        total = jnp.sum(ep, axis=-1, keepdims=True) + jnp.sum(es, axis=-1, keepdims=True)
        inv = 1.0 / total
        wp = (ep * inv).astype(jnp.bfloat16)
        ws = (es * inv).astype(jnp.bfloat16)
        acc = jnp.dot(wp, pv_ref[r0:, :], preferred_element_type=jnp.float32)
        acc = acc + jnp.dot(ws, sv_ref[:ns, :], preferred_element_type=jnp.float32)
        o_ref[r0:r0 + TQ, :] = jnp.where(qpos < n, acc, 0.0).astype(o_ref.dtype)


def attend(qkv, prefix, length):
    count = qkv.shape[0]
    pre = prefix.shape[0]
    grid_spec = pltpu.PrefetchScalarGridSpec(
        num_scalar_prefetch=1,
        grid=(H,),
        in_specs=[
            pl.BlockSpec((count, HD), lambda h, n: (0, h)),
            pl.BlockSpec((pre, HD), lambda h, n: (0, 0)),
            pl.BlockSpec((pre, HD), lambda h, n: (0, 1)),
            pl.BlockSpec((count, HD), lambda h, n: (0, H)),
            pl.BlockSpec((count, HD), lambda h, n: (0, H + 1)),
        ],
        out_specs=pl.BlockSpec((count, HD), lambda h, n: (0, h)),
    )
    flops = 4 * H * count * (pre + count) * HD
    return pl.pallas_call(
        _attn_kernel,
        out_shape=jax.ShapeDtypeStruct((count, H * HD), jnp.bfloat16),
        grid_spec=grid_spec,
        compiler_params=pltpu.CompilerParams(vmem_limit_bytes=48 * 1024 * 1024),
        cost_estimate=pl.CostEstimate(
            flops=flops,
            transcendentals=H * count * (pre + count),
            bytes_accessed=2 * (count * qkv.shape[1] + pre * prefix.shape[1] + count * H * HD),
        ),
    )(length.reshape(1).astype(jnp.int32), qkv, prefix, prefix, qkv, qkv)


def gather_by_a2a(piece, axis_name, count):
    spread = jnp.broadcast_to(piece[None], (count,) + piece.shape)
    return lax.all_to_all(spread, axis_name, 0, 0, tiled=True)


def shards(tokens, gain, w_qkv, prefix_kv, prefix_owner, suffix_len, slots):
    tok_dev = tokens.shape[0]
    n_grp = lax.axis_size("grp")
    n_shard = lax.axis_size("shard")
    core = lax.axis_index("grp") % 2
    pairs = [(g, g ^ 1) for g in range(n_grp)]

    owner = prefix_owner[0]
    sliced = gather_by_a2a(prefix_kv[0], "grp", n_grp)
    chosen = lax.dynamic_index_in_dim(sliced, owner, 0, keepdims=False)
    prefix = gather_by_a2a(chosen, "shard", n_shard).reshape(-1, chosen.shape[-1])

    order = slots.reshape(tok_dev)
    arrived = lax.all_to_all(tokens, "shard", 0, 0, tiled=True)
    order = lax.all_to_all(order, "shard", 0, 0, tiled=True)
    pos = order - lax.axis_index("shard") * tok_dev
    onehot = (jnp.arange(tok_dev, dtype=jnp.int32)[:, None] == pos[None, :]).astype(jnp.bfloat16)
    placed = jnp.dot(onehot, arrived, preferred_element_type=jnp.float32).astype(jnp.bfloat16)
    normed = normalize(placed, gain)

    d = w_qkv.shape[0]
    kh = d // 2
    w_mine = lax.dynamic_slice_in_dim(w_qkv, core * kh, kh, axis=0)
    w_rows = lax.all_gather(w_mine, "shard", axis=1, tiled=True)
    w_other = lax.ppermute(w_rows, "grp", pairs)
    n_mine = lax.dynamic_slice_in_dim(normed, core * kh, kh, axis=1)
    n_other = lax.dynamic_slice_in_dim(normed, (1 - core) * kh, kh, axis=1)
    acc = jnp.dot(n_mine, w_rows, preferred_element_type=jnp.float32)
    acc = acc + jnp.dot(n_other, w_other, preferred_element_type=jnp.float32)
    qkv = acc.astype(jnp.bfloat16)

    lengths = suffix_len.reshape(-1)
    return attend(qkv, prefix, lengths[0])


def solution(mesh):
    return jax.shard_map(
        shards,
        mesh=mesh,
        in_specs=(
            P(("grp", "shard"), None),
            P(),
            P(None, "shard"),
            P("grp", "shard", None),
            P("grp"),
            P("grp", "shard"),
            P("grp", "shard"),
        ),
        out_specs=P(("grp", "shard"), None),
        check_vma=False,
    )
```

time: 303 us -> 246 us (0.81)
  matrix products: 73.1 us -> 18.9 us
  local copies, waits for them, and re-layouts: 54.7 us -> 7.1 us
  Pallas kernels: 0 us -> 41 us
  blocking collectives: 0 us -> 32.7 us
  other arithmetic: 26.8 us -> 2.04 us
  starting transfers between devices: 20.9 us -> 8.19 us
  waiting for transfers between devices: 111 us -> 120 us
    dot_general x21 -> x2, matrix products: 69.5 us -> 15.6 us  [the longest x1 8.97 us: shards(): acc = acc + jnp.dot(n_other, w_other, preferred_element_type=jnp.float32)]
    pallas_call x0 -> x1, Pallas kernels: none -> 41 us  [attend(): pl.pallas_call(_attn_kernel, out_shape=jax.ShapeDtypeStruct((count, H * H...]
    all_to_all x0 -> x2, blocking collectives: none -> 32.7 us  [the longest x1 20.1 us: gather_by_a2a(): return lax.all_to_all(spread, axis_name, 0, 0, tiled=True)]
    all_to_all x2 -> x1, local copies, waits for them, and re-layouts: 13.1 us -> 0.09 us  [shards(): order = lax.all_to_all(order, 'shard', 0, 0, tiled=True)]
    all_to_all x2 -> x1, waiting for transfers between devices: 49.7 us -> 38.2 us  [shards(): arrived = lax.all_to_all(tokens, 'shard', 0, 0, tiled=True)]
    concatenate x1 -> x0, local copies, waits for them, and re-layouts: 11.2 us -> none  [shards(): jnp.concatenate([half0, half1], axis=2).reshape(tok_dev, n_shard * cols)]
    reduce_sum x11 -> x0, other arithmetic: 10.9 us -> none  [the longest x10 8.38 us: one_head(): jnp.sum(expd, axis=-1, keepdims=True)]
    all_gather x1, waiting for transfers between devices: 61.6 us -> 72.1 us  [shards(): w_rows = lax.all_gather(w_mine, 'shard', axis=1, tiled=True)]
  transfers between devices with their start and end apart: 7 -> 4, of which waited for: 3 -> 3; matrix products, arithmetic and copies ran while one was open for 16% -> 10% of each run, Pallas kernels for 0% -> 0%
where the time goes in v2:
time: 246 us; the launch traced here: 245 us
  waiting for transfers between devices  120 us (49%)
  Pallas kernels  41 us (17%)
  blocking collectives  32.7 us (13%)
  matrix products  18.9 us (8%)
  between operations  14.8 us (6%)
  starting transfers between devices  8.19 us (3%)
  local copies, waits for them, and re-layouts  7.1 us (3%)
    all_gather x1, waiting for transfers between devices, shards(): w_rows = lax.all_gather(w_mine, 'shard', axis=1, tiled=True)  72.1 us
    pallas_call x1, Pallas kernels, attend(): pl.pallas_call(_attn_kernel, out_shape=jax.ShapeDtypeStruct((count, H * H...  41 us
    all_to_all x1, waiting for transfers between devices, shards(): arrived = lax.all_to_all(tokens, 'shard', 0, 0, tiled=True)  38.2 us
    all_to_all x1, blocking collectives, gather_by_a2a(): return lax.all_to_all(spread, axis_name, 0, 0, tiled=True)  20.1 us
    all_to_all x1, blocking collectives, shards(): order = lax.all_to_all(order, 'shard', 0, 0, tiled=True)  12.6 us
    all_to_all x1, waiting for transfers between devices, gather_by_a2a(): return lax.all_to_all(spread, axis_name, 0, 0, tiled=True)  10.2 us
    dot_general x1, matrix products, shards(): acc = acc + jnp.dot(n_other, w_other, preferred_element_type=jnp.float32)  8.97 us
    dot_general x1, matrix products, shards(): acc = jnp.dot(n_mine, w_rows, preferred_element_type=jnp.float32)  6.61 us
  transfers between devices with their start and end apart: 4, of which 3 were waited for; matrix products, arithmetic and copies ran while one was open for 10% of the time, Pallas kernels for 0%

profile of v2, /device:TPU:0, one launch (start us, length us, event | category | flops | bytes accessed | tf_op | source)
XLA Modules:
  0.0 245.2 jit_solution(6576378703589676355)
XLA Ops:
  6.5 0.0 copy-start
  6.5 0.0 all-gather.2.cloned.1.call-start
  6.5 1.2 copy-done
  7.7 0.8 constant_dynamic-slice_fusion
  8.5 0.0 all-gather.2.cloned.1.call-update
  8.6 72.1 %all-gather.2.cloned.1.call-done = bf16[1280,3072]{0,1:T(8,128)(2,1)} async-done(((bf16[1280,192]{0,1:T(8,128)(2,1)}), bf16[1280,3072]{0,1:T(8,128)(2,1)}) %all-gather.2.cloned.1.call-update) | async-done | bytes 7864336 | tf_op jit(solution)/shard_map/all_gather | solution.py:110
  80.6 0.0 collective-permute-start
  80.6 0.5 broadcast.25
  81.1 1.3 reduce.7
  82.5 0.1 all_to_all.20
  82.6 12.6 %all_to_all.31 = s32[16,32,1]{1,2,0:T(1,128)S(1)} all-to-all(s32[16,32,1]{1,2,0:T(1,128)S(1)} %all_to_all.20), channel_id=1, replica_groups=mesh['grp'=8,'shard'=16] {'shard'}, dimensions={0} | all-to-all | bytes 4096 | tf_op jit(solution)/shard_map/all_to_all | solution.py:101
  95.2 1.0 broadcast_in_dim.9
  96.2 20.1 %all_to_all.32 = bf16[8,128,512]{2,1,0:T(8,128)(2,1)S(1)} all-to-all(bf16[8,128,512]{2,1,0:T(8,128)(2,1)S(1)} %broadcast_in_dim.9), channel_id=1, replica_groups=mesh['grp'=8,'shard'=16] {'grp'}, dimensions={0} | all-to-all | bytes 2097152 | tf_op jit(solution)/shard_map/all_to_all | solution.py:84
  116.3 4.5 %all-to-all-start.1 = ((bf16[16,32,2560]{2,1,0:T(8,128)(2,1)}), bf16[16,32,2560]{2,1,0:T(8,128)(2,1)}, u32[]{:S(2)}, u32[]{:S(2)}) async-start(bf16[16,32,2560]{2,1,0:T(8,128)(2,1)} %bitcast.17), calls=%async_computation.1 | async-start | bytes 5242880 | tf_op jit(solution)/shard_map/all_to_all | solution.py:100
  122.1 0.1 sub.18
  122.2 38.2 %all-to-all-done.1 = bf16[16,32,2560]{2,1,0:T(8,128)(2,1)} async-done(((bf16[16,32,2560]{2,1,0:T(8,128)(2,1)}), bf16[16,32,2560]{2,1,0:T(8,128)(2,1)}, u32[]{:S(2)}, u32[]{:S(2)}) %all-to-all-start.1) | async-done | bytes 2621472 | tf_op jit(solution)/shard_map/all_to_all | solution.py:100
  160.4 1.5 broadcast_in_dim.22
  161.9 3.7 %all-to-all-start.3 = ((bf16[16,128,512]{2,1,0:T(8,128)(2,1)}), bf16[16,128,512]{2,1,0:T(8,128)(2,1)S(1)}, u32[]{:S(2)}, u32[]{:S(2)}) async-start(bf16[16,128,512]{2,1,0:T(8,128)(2,1)} %broadcast_in_dim.22), calls=%async_computation.3 | async-start | bytes 4194304 | tf_op jit(solution)/shard_map/all_to_all | solution.py:84
  165.7 0.0 copy-start.2
  165.7 3.3 %fusion = (f32[512]{0:T(512)S(1)}, bf16[512,2560]{1,0:T(8,128)(2,1)S(1)}) fusion(bf16[512,2560]{1,0:T(8,128)(2,1)} %bitcast.2, s32[512]{0:T(512)S(1)} %sub.18), kind=kOutput, calls=%fused_computation.3 | convolution fusion | flops 1347681792 | bytes 5246976 | tf_op jit(solution)/shard_map/dot_general | solution.py:104
  169.0 0.0 copy-done.2
  169.1 0.7 fusion.2
  169.7 6.6 %fusion.4 = f32[512,3072]{1,0:T(8,128)S(1)} fusion(bf16[1280,3072]{0,1:T(8,128)(2,1)} %all-gather.2.cloned.1.call-done, bf16[512,2560]{1,0:T(8,128)(2,1)S(1)} %fusion.2, s32[]{:T(128)S(6)} %select_n.19), kind=kOutput, calls=%fused_computation.8 | convolution fusion | flops 4026531840 | bytes 15466500 | tf_op jit(solution)/shard_map/dot_general | solution.py:114
  176.3 0.0 collective-permute-done
  176.3 9.0 %add_convert_fusion.q_ref.sk_ref.sv_ref = bf16[512,3072]{1,0:T(8,128)(2,1)} fusion(f32[512,3072]{1,0:T(8,128)S(1)} %fusion.4, bf16[1280,3072]{0,1:T(8,128)(2,1)} %collective-permute-done, bf16[512,2560]{1,0:T(8,128)(2,1)S(1)} %fusion.2, s32[]{:T(128)S(6)} %select_n.20), kind=kOutput, calls=%fused_computation.2 | convolution fusion | flops 4029677568 | bytes 18612228 | tf_op jit(solution)/shard_map/dot_general | solution.py:115
  185.3 10.2 %all-to-all-done.3 = bf16[16,128,512]{2,1,0:T(8,128)(2,1)S(1)} async-done(((bf16[16,128,512]{2,1,0:T(8,128)(2,1)}), bf16[16,128,512]{2,1,0:T(8,128)(2,1)S(1)}, u32[]{:S(2)}, u32[]{:S(2)}) %all-to-all-start.3) | async-done | bytes 2097184 | tf_op jit(solution)/shard_map/all_to_all | solution.py:84
  195.5 0.0 copy-start.1
  195.5 1.9 copy-done.1
  197.4 41.0 %shard_map.73 = bf16[512,2560]{1,0:T(8,128)(2,1)} custom-call(s32[1]{0:T(128)} %bitcast.14.len_ref, bf16[512,3072]{1,0:T(8,128)(2,1)S(1)} %copy-done.1, bf16[2048,512]{1,0:T(8,128)(2,1)S(1)} %bitcast.15, bf16[2048,512]{1,0:T(8,128)(2,1)S(1)} %bitcast.16, bf16[512,3072]{1,0:T(8,128)(2,1)S(1)} %copy-done.1, bf16[512,3072]{1,0:T(8,128)(2,1)S(1)} %copy-done.1), custom_call_target="tpu_custom_call" | custom-call | flops 13421772800 | bytes 7864320 | tf_op jit(solution)/shard_map/pallas_call | solution.py:69
  (3 shorter events, 0.0 us)
Async XLA Ops:
  6.5 1.2 copy-start
  6.5 74.1 %all-gather.2.cloned.1.call-start = ((), (), s32[]{:S(2)}) async-start(), calls=%async_computation.4 | async-start | bytes 8355840 | tf_op jit(solution)/shard_map/all_gather | solution.py:110
  80.6 95.7 %collective-permute-start = (bf16[1280,3072]{0,1:T(8,128)(2,1)}, bf16[1280,3072]{0,1:T(8,128)(2,1)}, u32[]{:S(2)}, u32[]{:S(2)}) collective-permute-start(bf16[1280,3072]{0,1:T(8,128)(2,1)} %all-gather.2.cloned.1.call-done), channel_id=1, source_target_pairs={{0,16},{16,0},{32,48},{48,32},{64,80},{80,64},{96,112},{112,96},{1... | collective-permute-start | bytes 23592968 | tf_op jit(solution)/shard_map/ppermute | solution.py:111
  116.3 44.2 %all-to-all-start.1 = ((bf16[16,32,2560]{2,1,0:T(8,128)(2,1)}), bf16[16,32,2560]{2,1,0:T(8,128)(2,1)}, u32[]{:S(2)}, u32[]{:S(2)}) async-start(bf16[16,32,2560]{2,1,0:T(8,128)(2,1)} %bitcast.17), calls=%async_computation.1 | async-start | bytes 5242880 | tf_op jit(solution)/shard_map/all_to_all | solution.py:100
  161.9 33.5 %all-to-all-start.3 = ((bf16[16,128,512]{2,1,0:T(8,128)(2,1)}), bf16[16,128,512]{2,1,0:T(8,128)(2,1)S(1)}, u32[]{:S(2)}, u32[]{:S(2)}) async-start(bf16[16,128,512]{2,1,0:T(8,128)(2,1)} %broadcast_in_dim.22), calls=%async_computation.3 | async-start | bytes 4194304 | tf_op jit(solution)/shard_map/all_to_all | solution.py:84
  165.7 3.4 %copy-start.2 = (f32[2560]{0:T(1024)S(1)}, f32[2560]{0:T(1024)}, u32[]{:S(2)}) copy-start(f32[2560]{0:T(1024)} %param.8) | copy-start | bytes 30724
  195.5 1.9 copy-start.1
Sparse Core Ops, SparseCore 0:
  9.5 71.1 all-gather.1

commit v3 on v2

--- a/solution.py
+++ b/solution.py
@@ -5,11 +5,10 @@
 from jax.experimental.pallas import tpu as pltpu
 from jax.sharding import PartitionSpec as P
 
+
 H = 10
 HD = 256
 WINDOW = 2048
-SUF = 512
-HQ = 2560
 TQ = 128
 
 
@@ -96,12 +95,14 @@
     chosen = lax.dynamic_index_in_dim(sliced, owner, 0, keepdims=False)
     prefix = gather_by_a2a(chosen, "shard", n_shard).reshape(-1, chosen.shape[-1])
 
-    order = slots.reshape(tok_dev)
-    arrived = lax.all_to_all(tokens, "shard", 0, 0, tiled=True)
-    order = lax.all_to_all(order, "shard", 0, 0, tiled=True)
-    pos = order - lax.axis_index("shard") * tok_dev
+    here = slots.reshape(tok_dev, 1) % tok_dev
+    code = jnp.concatenate([here // 32, here % 32], axis=1).astype(tokens.dtype)
+    code = jnp.pad(code, ((0, 0), (0, 126)))
+    arrived = lax.all_to_all(jnp.concatenate([tokens, code], axis=1), "shard", 0, 0, tiled=True)
+    d = tokens.shape[1]
+    pos = arrived[:, d].astype(jnp.int32) * 32 + arrived[:, d + 1].astype(jnp.int32)
     onehot = (jnp.arange(tok_dev, dtype=jnp.int32)[:, None] == pos[None, :]).astype(jnp.bfloat16)
-    placed = jnp.dot(onehot, arrived, preferred_element_type=jnp.float32).astype(jnp.bfloat16)
+    placed = jnp.dot(onehot, arrived, preferred_element_type=jnp.float32).astype(jnp.bfloat16)[:, :d]
     normed = normalize(placed, gain)
 
     d = w_qkv.shape[0]

time: 246 us -> 234 us (0.951)
  blocking collectives: 32.7 us -> 0 us
  waiting for transfers between devices: 120 us -> 131 us
  starting transfers between devices: 8.19 us -> 13.4 us
  other arithmetic: 2.04 us -> 4.76 us
  local copies, waits for them, and re-layouts: 7.1 us -> 9.65 us
    all_to_all x2 -> x0, blocking collectives: 32.7 us -> none  [the longest x1 20.1 us: gather_by_a2a(): return lax.all_to_all(spread, axis_name, 0, 0, tiled=True)]
    all_to_all x1 -> x2, waiting for transfers between devices: 10.2 us -> 18.7 us  [gather_by_a2a(): return lax.all_to_all(spread, axis_name, 0, 0, tiled=True)]
    all_to_all x1 -> x2, starting transfers between devices: 3.72 us -> 8.12 us  [gather_by_a2a(): return lax.all_to_all(spread, axis_name, 0, 0, tiled=True)]
    concatenate x0 -> x2, other arithmetic: none -> 3.46 us  [the longest x1 3.45 us: shards(): jnp.concatenate([tokens, code], axis=1)]
  transfers between devices with their start and end apart: 4 -> 5, of which waited for: 3 -> 4; matrix products, arithmetic and copies ran while one was open for 10% -> 13% of each run, Pallas kernels for 0% -> 0%
where the time goes in v3:
time: 234 us
  waiting for transfers between devices  131 us (56%)
  Pallas kernels  41 us (18%)
  matrix products  19.6 us (8%)
  between operations  14.8 us (6%)
  starting transfers between devices  13.4 us (6%)
  local copies, waits for them, and re-layouts  9.65 us (4%)
  other arithmetic  4.76 us (2%)
    all_gather x1, waiting for transfers between devices, shards(): w_rows = lax.all_gather(w_mine, 'shard', axis=1, tiled=True)  72.1 us
    pallas_call x1, Pallas kernels, attend(): pl.pallas_call(_attn_kernel, out_shape=jax.ShapeDtypeStruct((count, H * H...  41 us
    all_to_all x1, waiting for transfers between devices, shards(): lax.all_to_all(jnp.concatenate([tokens, code], axis=1), 'shard', 0, 0, ti...  39.8 us
    all_to_all x2, waiting for transfers between devices, gather_by_a2a(): return lax.all_to_all(spread, axis_name, 0, 0, tiled=True)  18.7 us
    dot_general x1, matrix products, shards(): acc = acc + jnp.dot(n_other, w_other, preferred_element_type=jnp.float32)  9.88 us
    all_to_all x2, starting transfers between devices, gather_by_a2a(): return lax.all_to_all(spread, axis_name, 0, 0, tiled=True)  8.12 us
    dot_general x1, matrix products, shards(): acc = jnp.dot(n_mine, w_rows, preferred_element_type=jnp.float32)  6.13 us
    all_to_all x1, starting transfers between devices, shards(): lax.all_to_all(jnp.concatenate([tokens, code], axis=1), 'shard', 0, 0, ti...  5.3 us
  transfers between devices with their start and end apart: 5, of which 4 were waited for; matrix products, arithmetic and copies ran while one was open for 13% of the time, Pallas kernels for 0%

profile of v3, /device:TPU:0, one launch (start us, length us, event | category | flops | bytes accessed | tf_op | source)
XLA Modules:
  0.0 233.8 jit_solution(8364986965190461381)
XLA Ops:
  6.5 0.0 copy-start
  6.5 0.0 copy-start.3
  6.5 0.0 all-gather.2.cloned.1.call-start
  6.5 1.2 copy-done
  7.7 0.8 constant_dynamic-slice_fusion
  8.5 0.0 all-gather.2.cloned.1.call-update
  8.6 72.1 %all-gather.2.cloned.1.call-done = bf16[1280,3072]{0,1:T(8,128)(2,1)} async-done(((bf16[1280,192]{0,1:T(8,128)(2,1)}), bf16[1280,3072]{0,1:T(8,128)(2,1)}) %all-gather.2.cloned.1.call-update) | async-done | bytes 7864336 | tf_op jit(solution)/shard_map/all_gather | solution.py:111
  80.6 0.0 collective-permute-start
  80.6 2.0 broadcast_in_dim.9
  82.6 4.4 %all-to-all-start.1 = ((bf16[8,128,512]{2,1,0:T(8,128)(2,1)}), bf16[8,128,512]{2,1,0:T(8,128)(2,1)S(1)}, u32[]{:S(2)}, u32[]{:S(2)}) async-start(bf16[8,128,512]{2,1,0:T(8,128)(2,1)} %broadcast_in_dim.9), calls=%async_computation.1 | async-start | bytes 2097152 | tf_op jit(solution)/shard_map/all_to_all | solution.py:83
  87.0 0.0 copy-done.3
  87.1 0.2 copy.15
  87.3 3.5 %fusion.4 = bf16[512,2688]{1,0:T(8,128)(2,1)} fusion(bf16[512,2]{1,0:T(8,128)(2,1)S(1)} %copy.15, bf16[512,2560]{1,0:T(8,128)(2,1)} %param.7), kind=kLoop, calls=%fused_computation.9 | loop fusion | flops 8257536 | bytes 5376000 | tf_op jit(solution)/shard_map/concatenate | solution.py:101
  90.7 12.2 %all-to-all-done.1 = bf16[8,128,512]{2,1,0:T(8,128)(2,1)S(1)} async-done(((bf16[8,128,512]{2,1,0:T(8,128)(2,1)}), bf16[8,128,512]{2,1,0:T(8,128)(2,1)S(1)}, u32[]{:S(2)}, u32[]{:S(2)}) %all-to-all-start.1) | async-done | bytes 1048608 | tf_op jit(solution)/shard_map/all_to_all | solution.py:83
  102.9 5.3 %all-to-all-start = ((bf16[16,32,2688]{2,1,0:T(8,128)(2,1)}), bf16[16,32,2688]{2,1,0:T(8,128)(2,1)}, u32[]{:S(2)}, u32[]{:S(2)}) async-start(bf16[16,32,2688]{2,1,0:T(8,128)(2,1)} %bitcast.20), calls=%async_computation | async-start | bytes 5505024 | tf_op jit(solution)/shard_map/all_to_all | solution.py:101
  109.6 39.8 %all-to-all-done = bf16[16,32,2688]{2,1,0:T(8,128)(2,1)} async-done(((bf16[16,32,2688]{2,1,0:T(8,128)(2,1)}), bf16[16,32,2688]{2,1,0:T(8,128)(2,1)}, u32[]{:S(2)}, u32[]{:S(2)}) %all-to-all-start) | async-done | bytes 2752544 | tf_op jit(solution)/shard_map/all_to_all | solution.py:101
  149.3 1.5 broadcast_in_dim.22
  150.9 3.7 %all-to-all-start.2 = ((bf16[16,128,512]{2,1,0:T(8,128)(2,1)}), bf16[16,128,512]{2,1,0:T(8,128)(2,1)S(1)}, u32[]{:S(2)}, u32[]{:S(2)}) async-start(bf16[16,128,512]{2,1,0:T(8,128)(2,1)} %broadcast_in_dim.22), calls=%async_computation.2 | async-start | bytes 4194304 | tf_op jit(solution)/shard_map/all_to_all | solution.py:83
  154.6 1.1 fusion.15
  155.7 0.1 copy.13
  155.8 0.1 copy.14
  155.9 0.0 copy-start.2
  155.9 0.0 slice-start
  156.0 3.6 %fusion.8 = bf16[512,2688]{1,0:T(8,128)(2,1)S(1)} fusion(bf16[512,2688]{1,0:T(8,128)(2,1)} %bitcast.3, s32[512]{0:T(512)S(1)} %bitcast.22), kind=kOutput, calls=%fused_computation.14 | convolution fusion | flops 1409548288 | bytes 5507072 | tf_op jit(solution)/shard_map/dot_general | solution.py:105
  159.6 0.0 slice-start.1
  159.6 0.6 fusion.1
  160.2 0.0 copy-done.2
  160.2 0.7 fusion.3
  160.8 0.0 slice-done
  160.9 0.7 slice-done.1
  161.6 6.1 %fusion.6 = f32[512,3072]{1,0:T(8,128)} fusion(bf16[1280,3072]{0,1:T(8,128)(2,1)S(1)} %bitcast.24, bf16[512,2560]{1,0:T(8,128)(2,1)S(1)} %fusion.3, s32[]{:T(128)S(6)} %select_n.65), kind=kOutput, calls=%fused_computation.11 | convolution fusion | flops 4026531840 | bytes 15466500 | tf_op jit(solution)/shard_map/dot_general | solution.py:115
  167.7 0.0 collective-permute-done
  167.7 9.9 %add_convert_fusion.q_ref.sk_ref.sv_ref = bf16[512,3072]{1,0:T(8,128)(2,1)} fusion(f32[512,3072]{1,0:T(8,128)} %fusion.6, bf16[1280,3072]{0,1:T(8,128)(2,1)} %collective-permute-done, bf16[512,2560]{1,0:T(8,128)(2,1)S(1)} %fusion.3, s32[]{:T(128)S(6)} %select_n.66), kind=kOutput, calls=%fused_computation.2 | convolution fusion | flops 4029677568 | bytes 18612228 | tf_op jit(solution)/shard_map/dot_general | solution.py:116
  177.6 6.5 %all-to-all-done.2 = bf16[16,128,512]{2,1,0:T(8,128)(2,1)S(1)} async-done(((bf16[16,128,512]{2,1,0:T(8,128)(2,1)}), bf16[16,128,512]{2,1,0:T(8,128)(2,1)S(1)}, u32[]{:S(2)}, u32[]{:S(2)}) %all-to-all-start.2) | async-done | bytes 2097184 | tf_op jit(solution)/shard_map/all_to_all | solution.py:83
  184.1 0.0 copy-start.1
  184.1 1.9 copy-done.1
  186.0 41.0 %shard_map.73 = bf16[512,2560]{1,0:T(8,128)(2,1)} custom-call(s32[1]{0:T(128)} %bitcast.17.len_ref, bf16[512,3072]{1,0:T(8,128)(2,1)S(1)} %copy-done.1, bf16[2048,512]{1,0:T(8,128)(2,1)S(1)} %bitcast.18, bf16[2048,512]{1,0:T(8,128)(2,1)S(1)} %bitcast.19, bf16[512,3072]{1,0:T(8,128)(2,1)S(1)} %copy-done.1, bf16[512,3072]{1,0:T(8,128)(2,1)S(1)} %copy-done.1), custom_call_target="tpu_custom_call" | custom-call | flops 13421772800 | bytes 7864320 | tf_op jit(solution)/shard_map/pallas_call | solution.py:68
  (7 shorter events, 0.1 us)
Async XLA Ops:
  6.5 1.2 copy-start
  6.5 80.5 %copy-start.3 = (s32[1,512]{1,0:T(1,128)S(1)}, s32[1,512]{1,0:T(1,128)}, u32[]{:S(2)}) copy-start(s32[1,512]{1,0:T(1,128)} %param.13) | copy-start | bytes 6148
  6.5 74.1 %all-gather.2.cloned.1.call-start = ((), (), s32[]{:S(2)}) async-start(), calls=%async_computation.3 | async-start | bytes 8355840 | tf_op jit(solution)/shard_map/all_gather | solution.py:111
  80.6 87.1 %collective-permute-start = (bf16[1280,3072]{0,1:T(8,128)(2,1)}, bf16[1280,3072]{0,1:T(8,128)(2,1)}, u32[]{:S(2)}, u32[]{:S(2)}) collective-permute-start(bf16[1280,3072]{0,1:T(8,128)(2,1)} %all-gather.2.cloned.1.call-done), channel_id=1, source_target_pairs={{0,16},{16,0},{32,48},{48,32},{64,80},{80,64},{96,112},{112,96},{1... | collective-permute-start | bytes 23592968 | tf_op jit(solution)/shard_map/ppermute | solution.py:112
  82.6 20.3 %all-to-all-start.1 = ((bf16[8,128,512]{2,1,0:T(8,128)(2,1)}), bf16[8,128,512]{2,1,0:T(8,128)(2,1)S(1)}, u32[]{:S(2)}, u32[]{:S(2)}) async-start(bf16[8,128,512]{2,1,0:T(8,128)(2,1)} %broadcast_in_dim.9), calls=%async_computation.1 | async-start | bytes 2097152 | tf_op jit(solution)/shard_map/all_to_all | solution.py:83
  102.9 46.4 %all-to-all-start = ((bf16[16,32,2688]{2,1,0:T(8,128)(2,1)}), bf16[16,32,2688]{2,1,0:T(8,128)(2,1)}, u32[]{:S(2)}, u32[]{:S(2)}) async-start(bf16[16,32,2688]{2,1,0:T(8,128)(2,1)} %bitcast.20), calls=%async_computation | async-start | bytes 5505024 | tf_op jit(solution)/shard_map/all_to_all | solution.py:101
  150.9 33.2 %all-to-all-start.2 = ((bf16[16,128,512]{2,1,0:T(8,128)(2,1)}), bf16[16,128,512]{2,1,0:T(8,128)(2,1)S(1)}, u32[]{:S(2)}, u32[]{:S(2)}) async-start(bf16[16,128,512]{2,1,0:T(8,128)(2,1)} %broadcast_in_dim.22), calls=%async_computation.2 | async-start | bytes 4194304 | tf_op jit(solution)/shard_map/all_to_all | solution.py:83
  155.9 4.2 %copy-start.2 = (f32[2560]{0:T(1024)S(1)}, f32[2560]{0:T(1024)}, u32[]{:S(2)}) copy-start(f32[2560]{0:T(1024)} %param.8) | copy-start | bytes 30724
  155.9 4.9 %slice-start = ((s8[7864320]{0:T(1024)(128)(4,1)}), s8[4194304]{0:T(1024)(128)(4,1)S(1)}, s32[]{:S(2)}) async-start(s8[7864320]{0:T(1024)(128)(4,1)} %bitcast.23), calls=%async_computation.4 | async-start | bytes 8388608
  159.6 2.0 slice-start.1
  184.1 1.9 copy-start.1
Sparse Core Ops, SparseCore 0:
  9.5 71.1 all-gather.1
